TPU v7x, 256 devices: a whole 4x4x8 slice. The times are simulated.
256 devices in a mesh: blk: 128 (over z, x_hi, y, core), rows: 2 (over x_lo).
Axes of the slice: x: 4 (x_hi: 2, x_lo: 2; x = x_hi * 2 + x_lo), y: 4, z: 8, core: 2. Of those that a mesh axis runs over, the one named last changes fastest.
Arguments:
- tokens: bfloat16 [512, 8192], P(('blk', 'rows')), may hold values from -60 to 60
- norm_gain: float32 [8192], replicated, may hold values from 0.1 to 1.9
- gate_weight: bfloat16 [8192, 32768], P(None, 'blk'), may hold values from -0.09375 to 0.09375
- up_weight: bfloat16 [8192, 32768], P(None, 'blk'), may hold values from -0.09375 to 0.09375
- down_weight: bfloat16 [32768, 8192], P('blk'), may hold values from -0.046875 to 0.046875
- gate_mask: int32 [64, 256], P(None, 'blk'), may hold values from 0 to 1, as said below
- up_mask: int32 [64, 256], P(None, 'blk'), may hold values from 0 to 1, as said below
- down_mask: int32 [256, 64], P('blk'), may hold values 0 or 1
Outputs:
- ffn_out: bfloat16 [512, 8192], P(('blk', 'rows'))
Inputs may be any that keep to these rules, and one draw needn't show every extreme that they name: Each column of gate_mask (64 block flags) has between 16 and 48 ones, and some column has exactly 48. Each column of up_mask (64 block flags) has between 16 and 48 ones, and some column has exactly 48.
All inputs are finite; a program needn't handle non-finite values. No bound on the sum of `down_mask` on one device may be relied on, other than what follows from the above.
Results may differ from a plain program's by a relative error of at most 0.0065.
Values may be sent and summed in bfloat16 or wider, within the bound.
No kernel may reach another device: no remote copies, remote signals or barrier semaphores. Data moves between devices by JAX's collectives and lax.ppermute only.
A program may use at most 128 MiB of HBM per device.

v0:
```python
import jax
import jax.numpy as jnp
from jax import lax
from jax.sharding import PartitionSpec as P


def mask_blocks(weight, flags):
    height, width = weight.shape
    down_n = flags.shape[0]
    across_n = flags.shape[1]
    shaped = weight.reshape(down_n, height // down_n, across_n, width // across_n)
    return (shaped * flags.astype(weight.dtype)[:, None, :, None]).reshape(height, width)


def local(tokens, norm_gain, gate_weight, up_weight, down_weight, gate_mask, up_mask, down_mask):
    wide_tok = tokens.astype(jnp.float32)
    scale_inv = lax.rsqrt(jnp.mean(wide_tok * wide_tok, axis=-1, keepdims=True) + 1e-05)
    normed = (wide_tok * scale_inv * norm_gain).astype(jnp.bfloat16)
    gate_own, up_own, down_own = (gate_weight, up_weight, down_weight)
    gate_flags, up_flags, down_flags = (gate_mask, up_mask, down_mask)
    gate_kept = mask_blocks(gate_own, gate_flags)
    up_kept = mask_blocks(up_own, up_flags)
    down_kept = mask_blocks(down_own, down_flags)
    piece = lax.all_gather(normed, "blk", axis=0, tiled=True)
    gate = jnp.dot(piece, gate_kept, preferred_element_type=jnp.float32)
    up_val = jnp.dot(piece, up_kept, preferred_element_type=jnp.float32)
    hidden = (jax.nn.silu(gate) * up_val).astype(jnp.bfloat16)
    summed = lax.psum_scatter(
        jnp.dot(hidden, down_kept, preferred_element_type=jnp.float32),
        "blk",
        scatter_dimension=0,
        tiled=True,
    )
    return summed.astype(jnp.bfloat16)


def solution(mesh):
    return jax.shard_map(
        local,
        mesh=mesh,
        in_specs=(
            P(("blk", "rows"), None),
            P(),
            P(None, "blk"),
            P(None, "blk"),
            P("blk", None),
            P(None, "blk"),
            P(None, "blk"),
            P("blk", None),
        ),
        out_specs=P(("blk", "rows"), None),
        check_vma=False,
    )
```

profile of v0, /device:TPU:2, one launch (start us, length us, event | category | flops | bytes accessed | tf_op | source)
XLA Modules:
  0.0 906.0 jit_solution(3152752560273212439)
XLA Ops:
  6.5 0.0 all-gather.3.cloned.1.call-start
  6.5 0.9 fusion.8
  7.5 1.5 fusion.11
  9.0 0.0 all-gather.3.cloned.1.call-update
  9.0 0.7 convert_element_type.23
  9.7 0.1 copy.11
  9.8 0.7 convert_element_type.24
  10.5 0.1 copy.12
  10.6 0.7 convert_element_type.26
  11.3 1.3 dynamic-slice
  13.2 119.6 %all-gather.3.cloned.1.call-done = bf16[128,2,8192]{2,1,0:T(2,128)(2,1)} async-done(((bf16[1,2,8192]{2,1,0:T(2,128)(2,1)}), bf16[128,2,8192]{2,1,0:T(2,128)(2,1)}) %all-gather.3.cloned.1.call-update) | async-done | bytes 4194320 | tf_op jit(solution)/shard_map/all_gather | solution.py:24
  132.8 7.2 reshape.22
  140.0 0.0 copy-start
  140.0 2.2 mul.64
  142.2 0.0 copy-done
  142.2 3.5 fusion.4
  145.7 2.2 mul.68
  147.9 3.4 fusion.7
  151.3 0.0 copy-start.1
  151.4 1.1 mul.72
  152.5 1.1 copy-done.1
  153.5 6.5 fusion
  160.0 737.6 %all-reduce.2 = bf16[256,8192]{1,0:T(8,128)(2,1)} all-reduce(f32[256,8192]{1,0:T(8,128)} %fusion), channel_id=2, replica_groups=mesh['blk'=128,'rows'=2] {'blk'}, use_global_device_ids=true, to_apply=%region_1.2.clone | all-reduce | flops 2097152 | bytes 12582912
  897.6 1.6 dynamic-slice_convert_fusion
  (1 shorter events, 0.0 us)
Async XLA Ops:
  6.5 126.2 %all-gather.3.cloned.1.call-start = ((), (), s32[]{:S(2)}) async-start(), calls=%async_computation | async-start | bytes 4227072 | tf_op jit(solution)/shard_map/all_gather | solution.py:24
  140.0 2.2 copy-start
  151.3 2.2 copy-start.1
Sparse Core Ops, SparseCore 0:
  10.9 121.7 all-gather.2
where the time goes:
time: 907 us; the launch traced here: 906 us
  blocking collectives  738 us (81%)
  waiting for transfers between devices  120 us (13%)
  local copies, waits for them, and re-layouts  16.9 us (2%)
  between operations  14.1 us (2%)
  matrix products  13.4 us (1%)
    unnamed x1, blocking collectives  738 us
    all_gather x1, waiting for transfers between devices, local(): piece = lax.all_gather(normed, 'blk', axis=0, tiled=True)  120 us
  transfers between devices with their start and end apart: 1, of which 1 were waited for; matrix products, arithmetic and copies ran while one was open for 0% of the time, Pallas kernels for 0%

commit v1 on v0

--- a/solution.py
+++ b/solution.py
@@ -21,7 +21,8 @@
     gate_kept = mask_blocks(gate_own, gate_flags)
     up_kept = mask_blocks(up_own, up_flags)
     down_kept = mask_blocks(down_own, down_flags)
-    piece = lax.all_gather(normed, "blk", axis=0, tiled=True)
+    sent = jnp.stack([normed] * lax.axis_size("blk"))
+    piece = jnp.concatenate(lax.all_to_all(sent, "blk", 0, 0), axis=0)
     gate = jnp.dot(piece, gate_kept, preferred_element_type=jnp.float32)
     up_val = jnp.dot(piece, up_kept, preferred_element_type=jnp.float32)
     hidden = (jax.nn.silu(gate) * up_val).astype(jnp.bfloat16)

time: 907 us -> 884 us (0.975)
  waiting for transfers between devices: 120 us -> 95.7 us
  starting transfers between devices: 0.01 us -> 15.7 us
  between operations: 14.1 us -> 0.78 us
    all_gather x1 -> x0, waiting for transfers between devices: 120 us -> none  [local(): piece = lax.all_gather(normed, 'blk', axis=0, tiled=True)]
    all_to_all x0 -> x1, waiting for transfers between devices: none -> 95.7 us  [local(): piece = jnp.concatenate(lax.all_to_all(sent, 'blk', 0, 0), axis=0)]
    all_to_all x0 -> x1, starting transfers between devices: none -> 15.7 us  [local(): piece = jnp.concatenate(lax.all_to_all(sent, 'blk', 0, 0), axis=0)]
where the time goes in v1:
time: 884 us
  blocking collectives  734 us (83%)
  waiting for transfers between devices  95.7 us (11%)
  local copies, waits for them, and re-layouts  22.4 us (3%)
  starting transfers between devices  15.7 us (2%)
  matrix products  13.4 us (2%)
    unnamed x1, blocking collectives  734 us
    all_to_all x1, waiting for transfers between devices, local(): piece = jnp.concatenate(lax.all_to_all(sent, 'blk', 0, 0), axis=0)  95.7 us
  transfers between devices with their start and end apart: 1, of which 1 were waited for; matrix products, arithmetic and copies ran while one was open for 0% of the time, Pallas kernels for 0%

profile of v1, /device:TPU:2, one launch (start us, length us, event | category | flops | bytes accessed | tf_op | source)
XLA Modules:
  0.0 883.7 jit_solution(16467784680221409643)
XLA Ops:
  0.0 0.9 fusion.8
  0.9 0.9 fusion.10
  1.8 6.2 stack.2
  8.0 0.0 copy-start.2
  8.0 0.0 copy-start.3
  8.0 0.0 copy-start.4
  8.0 0.0 copy-start.5
  8.0 15.7 %all-to-all-start = ((bf16[128,2,8192]{2,1,0:T(2,128)(2,1)}), bf16[128,2,8192]{2,1,0:T(2,128)(2,1)}, u32[]{:S(2)}, u32[]{:S(2)}) async-start(bf16[128,2,8192]{2,1,0:T(2,128)(2,1)} %stack.2), calls=%async_computation | async-start | bytes 8388608 | tf_op jit(solution)/shard_map/all_to_all | solution.py:25
  23.8 0.0 copy-done.2
  23.8 0.1 copy.11
  23.9 0.0 copy-done.3
  23.9 0.1 copy.12
  24.0 0.0 copy-done.4
  24.0 0.0 copy-done.5
  24.0 0.6 dynamic-slice
  25.3 95.7 %all-to-all-done = bf16[128,2,8192]{2,1,0:T(2,128)(2,1)} async-done(((bf16[128,2,8192]{2,1,0:T(2,128)(2,1)}), bf16[128,2,8192]{2,1,0:T(2,128)(2,1)}, u32[]{:S(2)}, u32[]{:S(2)}) %all-to-all-start) | async-done | bytes 4194336 | tf_op jit(solution)/shard_map/all_to_all | solution.py:25
  121.0 7.2 reshape.26
  128.2 0.0 copy-start
  128.2 2.2 mul.64
  130.5 0.0 copy-done
  130.5 3.4 fusion.4
  133.9 2.2 mul.68
  136.2 3.5 fusion.7
  139.6 0.0 copy-start.1
  139.6 1.1 mul.72
  140.8 1.1 copy-done.1
  141.8 6.5 fusion
  148.3 733.9 %all-reduce.2 = bf16[256,8192]{1,0:T(8,128)(2,1)} all-reduce(f32[256,8192]{1,0:T(8,128)} %fusion), channel_id=2, replica_groups=mesh['blk'=128,'rows'=2] {'blk'}, use_global_device_ids=true, to_apply=%region_1.2.clone | all-reduce | flops 2097152 | bytes 12582912
  882.2 1.6 dynamic-slice_convert_fusion
  (4 shorter events, 0.0 us)
Async XLA Ops:
  8.0 15.8 %copy-start.2 = (s32[64,2]{0,1:T(2,128)S(1)}, s32[64,2]{0,1:T(2,128)}, u32[]{:S(2)}) copy-start(s32[64,2]{0,1:T(2,128)} %param.13) | copy-start | bytes 1540
  8.0 15.9 %copy-start.3 = (s32[64,2]{0,1:T(2,128)S(1)}, s32[64,2]{0,1:T(2,128)}, u32[]{:S(2)}) copy-start(s32[64,2]{0,1:T(2,128)} %param.14) | copy-start | bytes 1540
  8.0 16.0 %copy-start.4 = (s32[2,64]{1,0:T(2,128)S(1)}, s32[2,64]{1,0:T(2,128)}, u32[]{:S(2)}) copy-start(s32[2,64]{1,0:T(2,128)} %param.15) | copy-start | bytes 1540
  8.0 16.0 %copy-start.5 = (u32[256]{0:T(256)S(1)}, u32[256]{0:T(256)}, u32[]{:S(2)}) copy-start(u32[256]{0:T(256)} %constant.16) | copy-start | bytes 3076
  8.0 113.0 %all-to-all-start = ((bf16[128,2,8192]{2,1,0:T(2,128)(2,1)}), bf16[128,2,8192]{2,1,0:T(2,128)(2,1)}, u32[]{:S(2)}, u32[]{:S(2)}) async-start(bf16[128,2,8192]{2,1,0:T(2,128)(2,1)} %stack.2), calls=%async_computation | async-start | bytes 8388608 | tf_op jit(solution)/shard_map/all_to_all | solution.py:25
  128.2 2.2 copy-start
  139.6 2.2 copy-start.1
